TPU v7x, 32 devices: a whole 2x2x4 slice. The times are simulated.
32 devices in a mesh: wide: 4 (over y, core), narrow: 8 (over z, x).
Axes of the slice: x: 2, y: 2, z: 4, core: 2. Of those that a mesh axis runs over, the one named last changes fastest.
Arguments:
- tokens: bfloat16 [16384, 1024], P(('wide', 'narrow')), may hold values from -6 to 6
- cotangent: bfloat16 [16384, 1024], P(('wide', 'narrow')), may hold values from -6 to 6
- corpus_ids: int32 [8], P('wide'), may hold values from 0 to 7
- corpus_weights: float32 [8], replicated, may hold values from 0.3 to 3
- qkv_weight: bfloat16 [3, 1024, 1024], P(None, None, 'narrow'), may hold values from -0.1875 to 0.1875
- qkv_bias: float32 [3, 1024], P(None, 'narrow'), may hold values from -2 to 2
- out_weight: bfloat16 [1024, 1024], P('narrow'), may hold values from -0.75 to 0.75
- out_bias: float32 [1024], replicated, may hold values from -2 to 2
- up_weight: bfloat16 [1024, 4096], P(None, 'narrow'), may hold values from -0.1875 to 0.1875
- up_bias: float32 [4096], P('narrow'), may hold values from -3 to 3
- down_weight: bfloat16 [4096, 1024], P('narrow'), may hold values from -0.09375 to 0.09375
- down_bias: float32 [1024], replicated, may hold values from -2 to 2
- norm_gains: float32 [4, 1024], replicated, may hold values from 0.5 to 1.5
- norm_biases: float32 [4, 1024], replicated, may hold values from -2 to 2
Outputs:
- layer_out: bfloat16 [16384, 1024], P(('wide', 'narrow'))
- input_grad: bfloat16 [16384, 1024], P(('wide', 'narrow'))
- qkv_wgrad: float32 [3, 1024, 1024], P(None, None, 'narrow')
- qkv_bgrad: float32 [3, 1024], P(None, 'narrow')
- out_wgrad: float32 [1024, 1024], P('narrow')
- out_bgrad: float32 [1024], replicated
- up_wgrad: float32 [1024, 4096], P(None, 'narrow')
- up_bgrad: float32 [4096], P('narrow')
- down_wgrad: float32 [4096, 1024], P('narrow')
- down_bgrad: float32 [1024], replicated
- gain_grads: float32 [4, 1024], replicated
- bias_grads: float32 [4, 1024], replicated
All inputs are finite; a program needn't handle non-finite values.
Results may differ from a plain program's by a relative error of at most 0.023.
Values may be sent and summed in bfloat16 or wider, within the bound.
No kernel may reach another device: no remote copies, remote signals or barrier semaphores. Data moves between devices by JAX's collectives and lax.ppermute only.
A program may use at most 256 MiB of HBM per device.

v0:
```python
import math
import jax
import jax.numpy as jnp
from jax import lax
from jax.sharding import PartitionSpec as P

HEAD = 64
epsilon = 1e-05
root_half = 0.7071067811865476
gauss_norm = 0.3989422804014327
masked_score = -1e30


def norm_stats(vec_in):
    center = vec_in - jnp.mean(vec_in, axis=-1, keepdims=True)
    inverse = lax.rsqrt(jnp.mean(center * center, axis=-1, keepdims=True) + epsilon)
    return (center * inverse, inverse)


def norm_back(normed, inverse, gain_row, upstream):
    scaled = upstream * gain_row
    return inverse * (
        scaled
        - jnp.mean(scaled, axis=-1, keepdims=True)
        - normed * jnp.mean(scaled * normed, axis=-1, keepdims=True)
    )


def rotary_tables(length, head_size):
    half_size = head_size // 2
    inv_freq = jnp.exp(jnp.arange(half_size, dtype=jnp.float32) * (-math.log(10000.0) / half_size))
    angles = jnp.arange(length, dtype=jnp.float32)[:, None] * inv_freq[None, :]
    return (jnp.cos(angles), jnp.sin(angles))


def rotate(vectors, cos_table, sine_table):
    half_size = vectors.shape[-1] // 2
    front_half = vectors[..., :half_size]
    back_half = vectors[..., half_size:]
    cos_grid = cos_table[:, None, :]
    sin_grid = sine_table[:, None, :]
    return jnp.concatenate(
        [
            front_half * cos_grid - back_half * sin_grid,
            front_half * sin_grid + back_half * cos_grid,
        ],
        axis=-1,
    )


def rotate_back(vectors, cos_table, sine_table):
    half_size = vectors.shape[-1] // 2
    front_half = vectors[..., :half_size]
    back_half = vectors[..., half_size:]
    cos_grid = cos_table[:, None, :]
    sin_grid = sine_table[:, None, :]
    return jnp.concatenate(
        [
            front_half * cos_grid + back_half * sin_grid,
            back_half * cos_grid - front_half * sin_grid,
        ],
        axis=-1,
    )


def gelu_value(hidden):
    return 0.5 * hidden * (1.0 + lax.erf(hidden * root_half))


def gelu_slope(hidden):
    return (
        0.5 * (1.0 + lax.erf(hidden * root_half))
        + hidden * jnp.exp(-0.5 * hidden * hidden) * gauss_norm
    )


def project_qkv(gathered, qkv_weight, qkv_bias, cos_table, sine_table, seq_count, length):
    heads_here = qkv_weight.shape[2] // HEAD
    qkv_pre = (
        jnp.einsum("sd,tde->tse", gathered, qkv_weight, preferred_element_type=jnp.float32)
        + qkv_bias[:, None, :]
    )
    shaped = qkv_pre.reshape(3, seq_count, length, heads_here, HEAD)
    query = rotate(shaped[0], cos_table, sine_table).astype(jnp.bfloat16)
    key_rows = rotate(shaped[1], cos_table, sine_table).astype(jnp.bfloat16)
    values = shaped[2].astype(jnp.bfloat16)
    return (query, key_rows, values)


def block_scores(query, key_rows, block_start, block_rows):
    key_stop = block_start + block_rows
    query_block = query[:, block_start:key_stop]
    key_block = key_rows[:, :key_stop]
    scores = jnp.einsum(
        "bqhd,bkhd->bhqk", query_block, key_block, preferred_element_type=jnp.float32
    ) * (1.0 / math.sqrt(HEAD))
    query_pos = block_start + jnp.arange(block_rows)
    key_pos = jnp.arange(key_stop)
    allowed = key_pos[None, :] <= query_pos[:, None]
    return (jnp.where(allowed[None, None], scores, masked_score), query_block, key_block)


def attend_forward(query, key_rows, values, block_rows):
    length = query.shape[1]
    outputs = []
    totals = []
    for block_start in range(0, length, block_rows):
        key_stop = block_start + block_rows
        scores, query_block, key_block = block_scores(query, key_rows, block_start, block_rows)
        row_max = jnp.max(scores, axis=-1, keepdims=True)
        log_total = row_max + jnp.log(jnp.sum(jnp.exp(scores - row_max), axis=-1, keepdims=True))
        probs_low = jnp.exp(scores - log_total).astype(jnp.bfloat16)
        outputs.append(
            jnp.einsum(
                "bhqk,bkhd->bqhd",
                probs_low,
                values[:, :key_stop],
                preferred_element_type=jnp.float32,
            )
        )
        totals.append(log_total)
    return (jnp.concatenate(outputs, axis=1), totals)


def attend_backward(query, key_rows, values, attn_grad, totals, block_rows):
    length = query.shape[1]
    score_scale = 1.0 / math.sqrt(HEAD)
    keys_grad = jnp.zeros(key_rows.shape, jnp.float32)
    values_grad = jnp.zeros(values.shape, jnp.float32)
    query_grads = []
    for block_number, block_start in enumerate(range(0, length, block_rows)):
        key_stop = block_start + block_rows
        scores, query_block, key_block = block_scores(query, key_rows, block_start, block_rows)
        value_block = values[:, :key_stop]
        grad_block = attn_grad[:, block_start:key_stop]
        probs_full = jnp.exp(scores - totals[block_number])
        probs_low = probs_full.astype(jnp.bfloat16)
        probs_grad = jnp.einsum(
            "bqhd,bkhd->bhqk", grad_block, value_block, preferred_element_type=jnp.float32
        )
        row_dot = jnp.sum(probs_full * probs_grad, axis=-1, keepdims=True)
        scores_grad = (probs_full * (probs_grad - row_dot)).astype(jnp.bfloat16)
        query_grads.append(
            jnp.einsum(
                "bhqk,bkhd->bqhd", scores_grad, key_block, preferred_element_type=jnp.float32
            )
            * score_scale
        )
        pad_rows = ((0, 0), (0, length - key_stop), (0, 0), (0, 0))
        keys_grad = keys_grad + jnp.pad(
            jnp.einsum(
                "bhqk,bqhd->bkhd", scores_grad, query_block, preferred_element_type=jnp.float32
            )
            * score_scale,
            pad_rows,
        )
        values_grad = values_grad + jnp.pad(
            jnp.einsum(
                "bhqk,bqhd->bkhd", probs_low, grad_block, preferred_element_type=jnp.float32
            ),
            pad_rows,
        )
    return (jnp.concatenate(query_grads, axis=1), keys_grad, values_grad)


def shards(
    tokens,
    cotangent,
    corpus_ids,
    corpus_weights,
    qkv_weight,
    qkv_bias,
    out_weight,
    out_bias,
    up_weight,
    up_bias,
    down_weight,
    down_bias,
    norm_gains,
    norm_biases,
):
    shard_rows = tokens.shape[0]
    group_rows = shard_rows * lax.axis_size("narrow")
    seq_count = corpus_ids.shape[0]
    length = group_rows // seq_count
    block_rows = min(512, length)
    inner = qkv_weight.shape[2]
    first_row = lax.axis_index("narrow") * shard_rows
    cos_table, sine_table = rotary_tables(length, HEAD)
    layer_in = tokens.astype(jnp.float32)
    normed_first, inverse_first = norm_stats(layer_in)
    low_first = (normed_first * norm_gains[0] + norm_biases[0]).astype(jnp.bfloat16)
    gathered_first = lax.all_gather(low_first, "narrow", axis=0, tiled=True)
    query, key_rows, values = project_qkv(
        gathered_first, qkv_weight, qkv_bias, cos_table, sine_table, seq_count, length
    )
    attn_heads, totals = attend_forward(query, key_rows, values, block_rows)
    attn_low = attn_heads.reshape(group_rows, inner).astype(jnp.bfloat16)
    attn_rows = lax.all_to_all(attn_low, "narrow", 0, 1, tiled=True)
    out_full = lax.all_gather(out_weight, "narrow", axis=0, tiled=True)
    pre_attn = jnp.dot(attn_rows, out_full, preferred_element_type=jnp.float32) + out_bias
    normed_second, inverse_second = norm_stats(pre_attn)
    residual = layer_in + normed_second * norm_gains[1] + norm_biases[1]
    normed_third, inverse_third = norm_stats(residual)
    low_third = (normed_third * norm_gains[2] + norm_biases[2]).astype(jnp.bfloat16)
    gathered_third = lax.all_gather(low_third, "narrow", axis=0, tiled=True)
    hidden = jnp.dot(gathered_third, up_weight, preferred_element_type=jnp.float32) + up_bias
    act_low = gelu_value(hidden).astype(jnp.bfloat16)
    pre_mlp = (
        lax.psum_scatter(
            jnp.dot(act_low, down_weight, preferred_element_type=jnp.float32).astype(jnp.bfloat16),
            "narrow",
            scatter_dimension=0,
            tiled=True,
        ).astype(jnp.float32)
        + down_bias
    )
    normed_fourth, inverse_fourth = norm_stats(pre_mlp)
    final_sum = residual + normed_fourth * norm_gains[3] + norm_biases[3]
    layer_out = final_sum.astype(jnp.bfloat16)
    row_sequence = (first_row + jnp.arange(shard_rows, dtype=jnp.int32)) // length
    row_corpus = jnp.sum(
        jnp.where(
            row_sequence[:, None] == jnp.arange(seq_count, dtype=jnp.int32)[None, :],
            corpus_ids[None, :],
            0,
        ),
        axis=1,
    )
    row_weight = jnp.sum(
        jnp.where(
            row_corpus[:, None] == jnp.arange(corpus_weights.shape[0], dtype=jnp.int32)[None, :],
            corpus_weights[None, :],
            0.0,
        ),
        axis=1,
    )
    upstream = cotangent.astype(jnp.float32) * row_weight[:, None]
    mlp_grad = norm_back(normed_fourth, inverse_fourth, norm_gains[3], upstream).astype(
        jnp.bfloat16
    )
    mlp_full = lax.all_gather(mlp_grad, "narrow", axis=0, tiled=True)
    gathered_third = lax.all_gather(low_third, "narrow", axis=0, tiled=True)
    hidden = jnp.dot(gathered_third, up_weight, preferred_element_type=jnp.float32) + up_bias
    act_low = gelu_value(hidden).astype(jnp.bfloat16)
    down_wgrad = lax.dot_general(
        act_low, mlp_full, (((0,), (0,)), ((), ())), preferred_element_type=jnp.float32
    )
    act_grad = lax.dot_general(
        mlp_full, down_weight, (((1,), (1,)), ((), ())), preferred_element_type=jnp.float32
    )
    hidden_grad = (act_grad * gelu_slope(hidden)).astype(jnp.bfloat16)
    up_bgrad = jnp.sum(hidden_grad.astype(jnp.float32), axis=0)
    up_wgrad = lax.dot_general(
        gathered_third, hidden_grad, (((0,), (0,)), ((), ())), preferred_element_type=jnp.float32
    )
    rows_here = hidden_grad
    third_grad = lax.psum_scatter(
        lax.dot_general(
            rows_here, up_weight, (((1,), (1,)), ((), ())), preferred_element_type=jnp.float32
        ).astype(jnp.bfloat16),
        "narrow",
        scatter_dimension=0,
        tiled=True,
    ).astype(jnp.float32)
    residual_grad = upstream + norm_back(normed_third, inverse_third, norm_gains[2], third_grad)
    branch_grad = norm_back(normed_second, inverse_second, norm_gains[1], residual_grad).astype(
        jnp.bfloat16
    )
    gathered_first = lax.all_gather(low_first, "narrow", axis=0, tiled=True)
    query, key_rows, values = project_qkv(
        gathered_first, qkv_weight, qkv_bias, cos_table, sine_table, seq_count, length
    )
    attn_grad_rows = lax.dot_general(
        branch_grad, out_full, (((1,), (1,)), ((), ())), preferred_element_type=jnp.float32
    ).astype(jnp.bfloat16)
    attn_grad = lax.all_to_all(attn_grad_rows, "narrow", 1, 0, tiled=True)
    attn_grad = attn_grad.reshape(query.shape)
    query_grad, keys_grad, values_grad = attend_backward(
        query, key_rows, values, attn_grad, totals, block_rows
    )
    out_wgrad_rows = lax.dot_general(
        attn_rows, branch_grad, (((0,), (0,)), ((), ())), preferred_element_type=jnp.float32
    )
    out_wgrad = lax.psum_scatter(
        out_wgrad_rows.astype(jnp.bfloat16), "narrow", scatter_dimension=0, tiled=True
    )
    qkv_grad = jnp.stack(
        [
            rotate_back(query_grad, cos_table, sine_table),
            rotate_back(keys_grad, cos_table, sine_table),
            values_grad,
        ]
    )
    qkv_grad = qkv_grad.reshape(3, group_rows, inner).astype(jnp.bfloat16)
    qkv_bgrad = jnp.sum(qkv_grad.astype(jnp.float32), axis=1)
    qkv_wgrad = jnp.einsum(
        "sd,tse->tde", gathered_first, qkv_grad, preferred_element_type=jnp.float32
    )
    rows_here = qkv_grad
    first_grad = lax.psum_scatter(
        jnp.einsum("tse,tde->sd", rows_here, qkv_weight, preferred_element_type=jnp.float32).astype(
            jnp.bfloat16
        ),
        "narrow",
        scatter_dimension=0,
        tiled=True,
    ).astype(jnp.float32)
    input_grad = (
        residual_grad + norm_back(normed_first, inverse_first, norm_gains[0], first_grad)
    ).astype(jnp.bfloat16)
    gain_local = jnp.stack(
        [
            jnp.sum(first_grad * normed_first, axis=0),
            jnp.sum(residual_grad * normed_second, axis=0),
            jnp.sum(third_grad * normed_third, axis=0),
            jnp.sum(upstream * normed_fourth, axis=0),
        ]
    )
    bias_local = jnp.stack(
        [
            jnp.sum(first_grad, axis=0),
            jnp.sum(residual_grad, axis=0),
            jnp.sum(third_grad, axis=0),
            jnp.sum(upstream, axis=0),
        ]
    )
    out_blocal = jnp.sum(branch_grad.astype(jnp.float32), axis=0)
    down_blocal = jnp.sum(mlp_grad.astype(jnp.float32), axis=0)
    weight_sums = (
        lax.psum(qkv_wgrad.astype(jnp.bfloat16), "wide").astype(jnp.float32),
        lax.psum(qkv_bgrad.astype(jnp.bfloat16), "wide").astype(jnp.float32),
        lax.psum(out_wgrad, "wide").astype(jnp.float32),
        lax.psum(up_wgrad.astype(jnp.bfloat16), "wide").astype(jnp.float32),
        lax.psum(up_bgrad.astype(jnp.bfloat16), "wide").astype(jnp.float32),
        lax.psum(down_wgrad.astype(jnp.bfloat16), "wide").astype(jnp.float32),
    )
    small_sums = lax.psum((gain_local, bias_local, out_blocal, down_blocal), ("wide", "narrow"))
    return (
        layer_out,
        input_grad,
        weight_sums[0],
        weight_sums[1],
        weight_sums[2],
        small_sums[2],
        weight_sums[3],
        weight_sums[4],
        weight_sums[5],
        small_sums[3],
        small_sums[0],
        small_sums[1],
    )


def solution(mesh):
    return jax.shard_map(
        shards,
        mesh=mesh,
        in_specs=(
            P(("wide", "narrow"), None),
            P(("wide", "narrow"), None),
            P("wide"),
            P(),
            P(None, None, "narrow"),
            P(None, "narrow"),
            P("narrow", None),
            P(),
            P(None, "narrow"),
            P("narrow"),
            P("narrow", None),
            P(),
            P(),
            P(),
        ),
        out_specs=(
            P(("wide", "narrow"), None),
            P(("wide", "narrow"), None),
            P(None, None, "narrow"),
            P(None, "narrow"),
            P("narrow", None),
            P(),
            P(None, "narrow"),
            P("narrow"),
            P("narrow", None),
            P(),
            P(),
            P(),
        ),
        check_vma=False,
    )
```

profile of v0, /device:TPU:0, one launch (start us, length us, event | category | flops | bytes accessed | tf_op | source)
XLA Modules:
  0.0 1326.1 jit_solution(15998260063616890509)
XLA Ops:
  12.3 2.6 fusion.36
  19.9 122.4 %all-gather.5.cloned.1.call-done = bf16[4096,1024]{1,0:T(8,128)(2,1)} async-done(((bf16[512,1024]{1,0:T(8,128)(2,1)}), bf16[4096,1024]{1,0:T(8,128)(2,1)}) %all-gather.5.cloned.1.call-update) | async-done | bytes 8388624 | tf_op jit(solution)/shard_map/all_gather | solution.py:193
  142.3 7.1 add_bitcast_fusion
  152.9 5.0 reshape.335
  157.9 5.9 copy.105
  163.7 5.6 reshape.337
  169.3 5.7 reshape.336
  175.0 9.7 fusion.130
  184.7 6.4 copy.154
  191.2 6.4 copy.155
  197.6 10.1 fusion.129
  207.7 6.4 copy.156
  214.1 6.4 copy.157
  220.5 3.0 subtract_convert_fusion.2
  230.6 2.5 fusion.1
  233.1 3.5 exponential_reduce_fusion.1
  236.7 3.2 fusion.68
  239.9 4.3 fusion.70
  244.2 3.2 fusion
  247.5 4.3 exponential_reduce_fusion
  253.4 4.2 fusion.71
  260.9 3.6 all-to-all-start
  264.5 25.4 %all-to-all-done = bf16[8,512,128]{1,2,0:T(8,128)(2,1)S(1)} async-done(((bf16[8,512,128]{1,2,0:T(8,128)(2,1)}), bf16[8,512,128]{1,2,0:T(8,128)(2,1)S(1)}, u32[]{:S(2)}, u32[]{:S(2)}) %all-to-all-start) | async-done | bytes 1048608 | tf_op jit(solution)/shard_map/all_to_all | solution.py:199
  290.9 3.3 add_reduce_fusion
  299.3 123.4 %all-gather.9.cloned.1.call-done = bf16[4096,1024]{1,0:T(8,128)(2,1)} async-done(((bf16[512,1024]{1,0:T(8,128)(2,1)}), bf16[4096,1024]{1,0:T(8,128)(2,1)}) %all-gather.9.cloned.1.call-update) | async-done | bytes 8388624 | tf_op jit(solution)/shard_map/all_gather | solution.py:206
  422.7 10.0 multiply_convert_fusion.3
  434.7 6.7 convolution_convert_fusion.1
  442.1 145.0 %reduce-scatter.5.cloned.1.call-done = bf16[512,1024]{1,0:T(8,128)(2,1)} async-done(((bf16[4096,1024]{1,0:T(8,128)(2,1)}), bf16[512,1024]{1,0:T(8,128)(2,1)}) %reduce-scatter.5.cloned.1.call-update) | async-done | bytes 1048592 | tf_op jit(solution)/shard_map/reduce_scatter | solution.py:210
  590.5 3.3 multiply_reduce_fusion.4
  593.9 2.5 convert_reduce_fusion.3
  596.4 123.7 %all-gather.11.cloned.1.call-done = bf16[4096,1024]{1,0:T(8,128)(2,1)} async-done(((bf16[512,1024]{1,0:T(8,128)(2,1)}), bf16[4096,1024]{1,0:T(8,128)(2,1)}) %all-gather.11.cloned.1.call-update) | async-done | bytes 8388624 | tf_op jit(solution)/shard_map/all_gather | solution.py:242
  720.1 12.4 fusion.134
  734.5 7.3 convolution_convert_fusion
  741.8 145.8 %reduce-scatter.7.cloned.1.call-done = bf16[512,1024]{1,0:T(8,128)(2,1)} async-done(((bf16[4096,1024]{1,0:T(8,128)(2,1)}), bf16[512,1024]{1,0:T(8,128)(2,1)}) %reduce-scatter.7.cloned.1.call-update) | async-done | bytes 1048592 | tf_op jit(solution)/shard_map/reduce_scatter | solution.py:258
  887.6 4.7 fusion.48
  892.4 3.0 multiply_reduce_fusion.5
  900.4 3.7 all-to-all-start.1
  904.2 10.3 convolution_convert_fusion.3
  914.4 8.2 convolution_convert_fusion.4
  922.7 2.6 convolution_convert_fusion.2
  925.7 4.3 all-to-all-done.1
  932.5 4.6 convolution_bitcast_fusion.3
  942.8 3.4 convolution_bitcast_fusion.2
  946.2 5.5 multiply_reduce_fusion.2
  951.6 5.0 multiply_convert_fusion.2
  960.8 4.7 convolution_bitcast_fusion.1
  965.5 7.4 multiply_reduce_fusion.1
  972.9 10.6 multiply_convert_fusion.1
  985.9 2.8 fusion.63
  988.7 11.6 multiply_reduce_fusion
  1000.4 7.5 fusion.29
  1007.8 4.5 copy.144
  1014.2 12.4 multiply_convert_fusion
  1026.6 2.7 fusion.64
  1047.2 6.9 fusion.60
  1054.1 8.8 bitcast_convert_fusion
  1062.9 2.5 reduce_sum.374
  1065.4 6.5 all-reduce.7
  1073.1 48.5 %all-reduce.11.cloned.1.call-done = (bf16[3,1024,128]{1,2,0:T(8,128)(2,1)}, bf16[128,1024]{1,0:T(8,128)(2,1)}, bf16[1024,512]{1,0:T(8,128)(2,1)}, bf16[512,1024]{1,0:T(8,128)(2,1)}) async-done(((bf16[3,1024,128]{1,2,0:T(8,128)(2,1)}, bf16[128,1024]{1,0:T(8,128)(2,1)}, bf16[1024,512]{1,0:T(8,128)(2,1)}, bf16[512,1024]{1,0:T(8,128)(2,1)}), (bf16[3,1024,128]{1,2,0:T(8,128)(2,1)}, bf16[128,1024]{1,0:T(8,128)(2,1)}, ...) | async-done | bytes 3145744 | tf_op jit(solution)/shard_map/psum | solution.py:331
  1123.4 2.6 copy.135
  1126.1 2.9 convert_element_type.182
  1130.6 142.2 %reduce-scatter.9.cloned.1.call-done = bf16[512,1024]{1,0:T(8,128)(2,1)} async-done(((bf16[4096,1024]{1,0:T(8,128)(2,1)}), bf16[512,1024]{1,0:T(8,128)(2,1)}) %reduce-scatter.9.cloned.1.call-update) | async-done | bytes 1048592 | tf_op jit(solution)/shard_map/reduce_scatter | solution.py:301
  1275.2 40.3 %all-reduce.6 = (f32[1024]{0:T(1024)}, f32[1024]{0:T(1024)}, f32[4,1024]{1,0:T(4,128)}, f32[4,1024]{1,0:T(4,128)}) all-reduce(f32[1024]{0:T(1024)S(1)} %copy-done.74, f32[1024]{0:T(1024)S(1)} %copy-done.70, f32[4,1024]{1,0:T(4,128)S(1)} %pad_maximum_fusion.9, ...), channel_id=1, replica_groups=mesh['wide'=4,'narrow'=8] {'wide','narrow'}, use_global_device_ids=true, to_apply=%region_39.40 | all-reduce | flops 10240 | bytes 81920 | tf_op jit(solution)/shard_map/psum | solution.py:338
  1315.5 3.6 fusion.40
  (302 shorter events, 86.1 us)
Async XLA Ops:
  7.2 415.5 %copy-start = (bf16[1024,512]{1,0:T(8,128)(2,1)S(1)}, bf16[1024,512]{1,0:T(8,128)(2,1)}, u32[]{:S(2)}) copy-start(bf16[1024,512]{1,0:T(8,128)(2,1)} %param.22) | copy-start | bytes 3145732
  7.2 135.1 %copy-start.82 = (f32[3,128]{1,0:T(4,128)S(1)}, f32[3,128]{1,0:T(4,128)}, u32[]{:S(2)}) copy-start(f32[3,128]{1,0:T(4,128)} %param.19) | copy-start | bytes 4612
  7.2 135.1 %all-gather.5.cloned.1.call-start = ((), (), s32[]{:S(2)}) async-start(), calls=%async_computation.6 | async-start | bytes 9437184 | tf_op jit(solution)/shard_map/all_gather | solution.py:193
  14.9 249.6 %all-gather.7.cloned.1.call-start = ((), (), s32[]{:S(2)}) async-start(), calls=%async_computation.7 | async-start | bytes 2359296 | tf_op jit(solution)/shard_map/all_gather | solution.py:200
  16.9 219.8 %copy-start.21 = (pred[512,1024]{1,0:T(8,128)(4,1)}, pred[512,1024]{1,0:T(8,128)(4,1)S(1)}, u32[]{:S(2)}) copy-start(pred[512,1024]{1,0:T(8,128)(4,1)S(1)} %iota_compare_fusion.2) | copy-start | bytes 1572868
  19.2 220.7 %copy-start.14 = (pred[512,1536]{1,0:T(8,128)(4,1)}, pred[512,1536]{1,0:T(8,128)(4,1)S(1)}, u32[]{:S(2)}) copy-start(pred[512,1536]{1,0:T(8,128)(4,1)S(1)} %iota_compare_fusion.1) | copy-start | bytes 2359300
  19.9 233.1 %copy-start.10 = (pred[512,2048]{1,0:T(8,128)(4,1)}, pred[512,2048]{1,0:T(8,128)(4,1)S(1)}, u32[]{:S(2)}) copy-start(pred[512,2048]{1,0:T(8,128)(4,1)S(1)} %iota_compare_fusion) | copy-start | bytes 3145732
  223.5 7.0 copy-start.16
  223.5 7.0 copy-start.18
  223.5 20.7 %copy-start.23 = (bf16[2,2048,2,32]{1,3,2,0:T(8,128)(2,1)}, bf16[2,2048,2,32]{1,3,2,0:T(8,128)(2,1)S(1)}, u32[]{:S(2)}) copy-start(bf16[2,2048,2,32]{1,3,2,0:T(8,128)(2,1)S(1)} %get-tuple-element.103) | copy-start | bytes 1572868
  223.6 20.7 %copy-start.27 = (bf16[2,2048,2,32]{1,3,2,0:T(8,128)(2,1)}, bf16[2,2048,2,32]{1,3,2,0:T(8,128)(2,1)S(1)}, u32[]{:S(2)}) copy-start(bf16[2,2048,2,32]{1,3,2,0:T(8,128)(2,1)S(1)} %get-tuple-element.104) | copy-start | bytes 1572868
  225.4 26.4 %copy-start.5 = (f32[2,2,512,512]{2,3,1,0:T(8,128)}, f32[2,2,512,512]{2,3,1,0:T(8,128)S(1)}, u32[]{:S(2)}) copy-start(f32[2,2,512,512]{2,3,1,0:T(8,128)S(1)} %get-tuple-element.133) | copy-start | bytes 12582916
  228.1 8.6 copy-start.4
  233.1 6.8 copy-start.3
  247.4 6.0 copy-start.2
  257.8 33.1 %copy-start.61 = (f32[1024]{0:T(1024)S(1)}, f32[1024]{0:T(1024)}, u32[]{:S(2)}) copy-start(f32[1024]{0:T(1024)} %param.21) | copy-start | bytes 12292
  260.9 29.0 %all-to-all-start = ((bf16[8,512,128]{1,2,0:T(8,128)(2,1)}), bf16[8,512,128]{1,2,0:T(8,128)(2,1)S(1)}, u32[]{:S(2)}, u32[]{:S(2)}) async-start(bf16[8,512,128]{1,2,0:T(8,128)(2,1)} %copy.117), calls=%async_computation | async-start | bytes 2097152 | tf_op jit(solution)/shard_map/all_to_all | solution.py:199
  264.5 158.2 %all-gather.9.cloned.1.call-start = ((), (), s32[]{:S(2)}) async-start(), calls=%async_computation.8 | async-start | bytes 9437184 | tf_op jit(solution)/shard_map/all_gather | solution.py:206
  296.5 126.1 %copy-start.83 = (f32[512]{0:T(512)S(1)}, f32[512]{0:T(512)}, u32[]{:S(2)}) copy-start(f32[512]{0:T(512)} %param.23) | copy-start | bytes 6148
  299.3 287.9 %reduce-scatter.5.cloned.1.call-start = ((), (), s32[]{:S(2)}) async-start(), calls=%async_computation.9 | async-start | bytes 9437184 | tf_op jit(solution)/shard_map/reduce_scatter | solution.py:210
  422.7 12.0 copy-start.80
  441.3 145.8 %copy-start.62 = (f32[1024]{0:T(1024)S(1)}, f32[1024]{0:T(1024)}, u32[]{:S(2)}) copy-start(f32[1024]{0:T(1024)} %param.25) | copy-start | bytes 12292
  441.3 278.7 %all-gather.11.cloned.1.call-start = ((), (), s32[]{:S(2)}) async-start(), calls=%async_computation.10 | async-start | bytes 9437184 | tf_op jit(solution)/shard_map/all_gather | solution.py:242
  587.2 6.7 copy-start.12
  587.2 6.7 copy-start.36
  596.4 291.3 %reduce-scatter.7.cloned.1.call-start = ((), (), s32[]{:S(2)}) async-start(), calls=%async_computation.11 | async-start | bytes 9437184 | tf_op jit(solution)/shard_map/reduce_scatter | solution.py:258
  741.8 145.8 %copy-start.13 = (bf16[512,1024]{1,0:T(8,128)(2,1)S(1)}, bf16[512,1024]{1,0:T(8,128)(2,1)}, u32[]{:S(2)}) copy-start(bf16[512,1024]{1,0:T(8,128)(2,1)} %reduce-scatter.5.cloned.1.call-done) | copy-start | bytes 3145732
  887.6 4.7 copy-start.37
  887.6 4.7 copy-start.43
  900.4 29.6 %all-to-all-start.1 = ((bf16[512,8,128]{0,2,1:T(8,128)(2,1)}), bf16[512,8,128]{0,2,1:T(8,128)(2,1)S(1)}, u32[]{:S(2)}, u32[]{:S(2)}) async-start(bf16[512,8,128]{0,2,1:T(8,128)(2,1)} %bitcast.16), calls=%async_computation.3 | async-start | bytes 2097152 | tf_op jit(solution)/shard_map/all_to_all | solution.py:277
  904.1 150.0 %reduce-scatter.11.cloned.1.call-start = ((), (), s32[]{:S(2)}) async-start(), calls=%async_computation.13 | async-start | bytes 2359296 | tf_op jit(solution)/shard_map/reduce_scatter | solution.py:285
  904.1 10.3 copy-start.86
  914.4 8.3 copy-start.41
  914.4 8.3 copy-start.58
  925.3 196.3 %all-reduce.11.cloned.1.call-start = ((), (), s32[]{:S(2)}) async-start(), calls=%async_computation.14 | async-start | bytes 6291456 | tf_op jit(solution)/shard_map/psum | solution.py:331
  931.0 6.0 copy-start.6
  931.0 6.0 copy-start.33
  937.1 5.7 slice-start.7
  951.6 5.1 copy-start.24
  951.6 5.1 copy-start.28
  951.6 9.1 slice-start.4
  951.6 9.1 slice-start.5
  972.9 15.8 %slice-start = ((s8[16777216]{0:T(1024)(128)(4,1)}), s8[4194304]{0:T(1024)(128)(4,1)S(1)}, s32[]{:S(2)}) async-start(s8[16777216]{0:T(1024)(128)(4,1)} %bitcast.116), calls=%async_computation.15 | async-start | bytes 8388608
  972.9 15.8 %slice-start.1 = ((s8[16777216]{0:T(1024)(128)(4,1)}), s8[4194304]{0:T(1024)(128)(4,1)S(1)}, s32[]{:S(2)}) async-start(s8[16777216]{0:T(1024)(128)(4,1)} %bitcast.116), calls=%async_computation.16 | async-start | bytes 8388608
  972.9 15.8 %slice-start.2 = ((s8[16777216]{0:T(1024)(128)(4,1)}), s8[4194304]{0:T(1024)(128)(4,1)S(1)}, s32[]{:S(2)}) async-start(s8[16777216]{0:T(1024)(128)(4,1)} %bitcast.116), calls=%async_computation.17 | async-start | bytes 8388608
  983.5 5.2 slice-start.3
  1007.8 6.3 copy-start.69
  1014.2 12.4 copy-start.26
  1014.2 12.4 copy-start.30
  1047.2 7.0 copy-start.81
  1054.1 218.7 %reduce-scatter.9.cloned.1.call-start = ((), (), s32[]{:S(2)}) async-start(), calls=%async_computation.12 | async-start | bytes 9437184 | tf_op jit(solution)/shard_map/reduce_scatter | solution.py:301
  1121.6 7.4 copy-start.54
  1123.4 149.3 %copy-start.9 = (bf16[512,1024]{1,0:T(8,128)(2,1)S(1)}, bf16[512,1024]{1,0:T(8,128)(2,1)}, u32[]{:S(2)}) copy-start(bf16[512,1024]{1,0:T(8,128)(2,1)} %param.14) | copy-start | bytes 3145732
  1123.4 149.3 %copy-start.64 = (f32[1,1024]{1,0:T(1,128)S(1)}, f32[1,1024]{1,0:T(1,128)}, u32[]{:S(2)}) copy-start(f32[1,1024]{1,0:T(1,128)} %copy-done.63) | copy-start | bytes 12292
  1123.4 149.3 %copy-start.66 = (f32[512]{0:T(512)S(1)}, f32[512]{0:T(512)}, u32[]{:S(2)}) copy-start(f32[512]{0:T(512)} %copy-done.65) | copy-start | bytes 6148
  1123.4 149.3 %copy-start.68 = (f32[512]{0:T(512)S(1)}, f32[512]{0:T(512)}, u32[]{:S(2)}) copy-start(f32[512]{0:T(512)} %copy-done.67) | copy-start | bytes 6148
  1126.1 148.9 %copy-start.72 = (f32[1024]{0:T(1024)S(1)}, f32[1024]{0:T(1024)}, u32[]{:S(2)}) copy-start(f32[1024]{0:T(1024)} %get-tuple-element.64) | copy-start | bytes 12292
  1126.1 149.0 %copy-start.73 = (f32[1024]{0:T(1024)S(1)}, f32[1024]{0:T(1024)}, u32[]{:S(2)}) copy-start(f32[1024]{0:T(1024)} %get-tuple-element.60) | copy-start | bytes 12292
  1126.1 149.0 %copy-start.76 = (f32[1024]{0:T(1024)S(1)}, f32[1024]{0:T(1024)}, u32[]{:S(2)}) copy-start(f32[1024]{0:T(1024)} %get-tuple-element.62) | copy-start | bytes 12292
  1126.1 149.0 %copy-start.71 = (f32[1024]{0:T(1024)S(1)}, f32[1024]{0:T(1024)}, u32[]{:S(2)}) copy-start(f32[1024]{0:T(1024)} %get-tuple-element.73) | copy-start | bytes 12292
  1126.1 149.0 %copy-start.75 = (f32[1024]{0:T(1024)S(1)}, f32[1024]{0:T(1024)}, u32[]{:S(2)}) copy-start(f32[1024]{0:T(1024)} %get-tuple-element.75) | copy-start | bytes 12292
  1126.1 149.0 %copy-start.70 = (f32[1024]{0:T(1024)S(1)}, f32[1024]{0:T(1024)}, u32[]{:S(2)}) copy-start(f32[1024]{0:T(1024)} %get-tuple-element.86) | copy-start | bytes 12292
  1126.1 149.0 %copy-start.74 = (f32[1024]{0:T(1024)S(1)}, f32[1024]{0:T(1024)}, u32[]{:S(2)}) copy-start(f32[1024]{0:T(1024)} %get-tuple-element.88) | copy-start | bytes 12292
  1129.0 190.1 %copy-start.1 = (bf16[1024,512]{1,0:T(8,128)(2,1)S(1)}, bf16[1024,512]{1,0:T(8,128)(2,1)}, u32[]{:S(2)}) copy-start(bf16[1024,512]{1,0:T(8,128)(2,1)} %param.22) | copy-start | bytes 3145732
  (43 other events, 108.2 us)
Sparse Core Ops, SparseCore 0:
  15.0 127.2 all-gather.4
  144.4 47.2 all-gather.6
  299.4 123.2 all-gather.8
  441.5 145.6 reduce-scatter.4
  596.5 123.5 all-gather.10
  742.0 145.6 reduce-scatter.6
  925.4 69.7 reduce-scatter.10
  1054.2 67.3 all-reduce.10
  1125.2 147.5 reduce-scatter.8
where the time goes:
time: 1340 us; the launch traced here: 1330 us
  waiting for transfers between devices  881 us (66%)
  matrix products  168 us (13%)
  local copies, waits for them, and re-layouts  110 us (8%)
  other arithmetic  96.1 us (7%)
  blocking collectives  46.8 us (3%)
  between operations  15.4 us (1%)
    reduce_scatter x1, waiting for transfers between devices, shards(): lax.psum_scatter(lax.dot_general(rows_here, up_weight, (((1,), (1,)), (()...  146 us
    reduce_scatter x1, waiting for transfers between devices, shards(): lax.psum_scatter(jnp.dot(act_low, down_weight, preferred_element_type=jnp...  145 us
    reduce_scatter x1, waiting for transfers between devices, shards(): lax.psum_scatter(jnp.einsum('tse,tde->sd', rows_here, qkv_weight, preferr...  142 us
    all_gather x1, waiting for transfers between devices, shards(): mlp_full = lax.all_gather(mlp_grad, 'narrow', axis=0, tiled=True)  124 us
    all_gather x1, waiting for transfers between devices, shards(): gathered_third = lax.all_gather(low_third, 'narrow', axis=0, tiled=True)  123 us
    all_gather x1, waiting for transfers between devices, shards(): gathered_first = lax.all_gather(low_first, 'narrow', axis=0, tiled=True)  122 us
    psum x1, waiting for transfers between devices, shards(): lax.psum(qkv_wgrad.astype(jnp.bfloat16), 'wide').astype(jnp.float32)  48.5 us
    unnamed x199, local copies, waits for them, and re-layouts  42.6 us
  transfers between devices with their start and end apart: 11, of which 9 were waited for; matrix products, arithmetic and copies ran while one was open for 21% of the time, Pallas kernels for 0%

commit v1 on v0

--- a/solution.py
+++ b/solution.py
@@ -190,7 +190,15 @@
     layer_in = tokens.astype(jnp.float32)
     normed_first, inverse_first = norm_stats(layer_in)
     low_first = (normed_first * norm_gains[0] + norm_biases[0]).astype(jnp.bfloat16)
-    gathered_first = lax.all_gather(low_first, "narrow", axis=0, tiled=True)
+    ways, here, lap = (lax.axis_size("narrow"), lax.axis_index("narrow"), low_first.shape[0])
+    line, have = (low_first, 1)
+    while have < ways:
+        line = jnp.concatenate(
+            [line, lax.ppermute(line, "narrow", [(d, (d - have) % ways) for d in range(ways)])],
+            axis=0,
+        )
+        have = 2 * have
+    gathered_first = jnp.roll(line, here * lap, axis=0)
     query, key_rows, values = project_qkv(
         gathered_first, qkv_weight, qkv_bias, cos_table, sine_table, seq_count, length
     )

time: 1340 us -> 1670 us (1.25)
  waiting for transfers between devices: 881 us -> 1070 us
  local copies, waits for them, and re-layouts: 110 us -> 206 us
  matrix products: 168 us -> 202 us
    ppermute x0 -> x3, waiting for transfers between devices: none -> 347 us  [shards(): lax.ppermute(line, 'narrow', [(d, (d - have) % ways) for d in range(ways)])]
    all_gather x1, waiting for transfers between devices: 122 us -> 0.01 us  [shards(): gathered_first = lax.all_gather(low_first, 'narrow', axis=0, tiled=True)]
    unnamed x199 -> x223, local copies, waits for them, and re-layouts: 42.6 us -> 84 us
    reduce_scatter x1, waiting for transfers between devices: 146 us -> 114 us  [shards(): lax.psum_scatter(lax.dot_general(rows_here, up_weight, (((1,), (1,)), (()...]
    dot_general x4 -> x8, matrix products: 8.36 us -> 33.9 us  [block_scores(): jnp.einsum('bqhd,bkhd->bhqk', query_block, key_block, preferred_element_t...]
    slice x2 -> x4, local copies, waits for them, and re-layouts: 19.8 us -> 39.5 us  [rotate(): front_half = vectors[..., :half_size]]
  transfers between devices with their start and end apart: 11 -> 14, of which waited for: 9 -> 11; matrix products, arithmetic and copies ran while one was open for 21% -> 25% of each run, Pallas kernels for 0% -> 0%
where the time goes in v1:
time: 1670 us; the launch traced here: 1660 us
  waiting for transfers between devices  1070 us (64%)
  local copies, waits for them, and re-layouts  206 us (12%)
  matrix products  202 us (12%)
  other arithmetic  101 us (6%)
  blocking collectives  46.8 us (3%)
    ppermute x3, waiting for transfers between devices, shards(): lax.ppermute(line, 'narrow', [(d, (d - have) % ways) for d in range(ways)])  347 us
    reduce_scatter x1, waiting for transfers between devices, shards(): lax.psum_scatter(jnp.dot(act_low, down_weight, preferred_element_type=jnp...  145 us
    reduce_scatter x1, waiting for transfers between devices, shards(): lax.psum_scatter(jnp.einsum('tse,tde->sd', rows_here, qkv_weight, preferr...  142 us
    all_gather x1, waiting for transfers between devices, shards(): mlp_full = lax.all_gather(mlp_grad, 'narrow', axis=0, tiled=True)  124 us
    all_gather x1, waiting for transfers between devices, shards(): gathered_third = lax.all_gather(low_third, 'narrow', axis=0, tiled=True)  123 us
    reduce_scatter x1, waiting for transfers between devices, shards(): lax.psum_scatter(lax.dot_general(rows_here, up_weight, (((1,), (1,)), (()...  114 us
    unnamed x223, local copies, waits for them, and re-layouts  84 us
    psum x1, waiting for transfers between devices, shards(): lax.psum(qkv_wgrad.astype(jnp.bfloat16), 'wide').astype(jnp.float32)  48.6 us
  transfers between devices with their start and end apart: 14, of which 11 were waited for; matrix products, arithmetic and copies ran while one was open for 25% of the time, Pallas kernels for 0%

profile of v1, /device:TPU:0, one launch (start us, length us, event | category | flops | bytes accessed | tf_op | source)
XLA Modules:
  0.0 1661.3 jit_solution(12252595174355461433)
XLA Ops:
  16.5 6.1 collective-permute-start
  22.5 40.6 %collective-permute-done = bf16[512,1024]{1,0:T(8,128)(2,1)S(1)} collective-permute-done((bf16[512,1024]{1,0:T(8,128)(2,1)}, bf16[512,1024]{1,0:T(8,128)(2,1)S(1)}, u32[]{:S(2)}, u32[]{:S(2)}) %collective-permute-start) | collective-permute-done | bytes 1048608 | tf_op jit(solution)/shard_map/ppermute | solution.py:197
  65.1 58.8 %collective-permute-done.1 = bf16[1024,1024]{1,0:T(8,128)(2,1)S(1)} collective-permute-done((bf16[1024,1024]{1,0:T(8,128)(2,1)S(1)}, bf16[1024,1024]{1,0:T(8,128)(2,1)S(1)}, u32[]{:S(2)}, u32[]{:S(2)}) %collective-permute-start.1) | collective-permute-done | bytes 2097184 | tf_op jit(solution)/shard_map/ppermute | solution.py:197
  138.4 247.3 %collective-permute-done.2 = bf16[2048,1024]{1,0:T(8,128)(2,1)} collective-permute-done((bf16[2048,1024]{1,0:T(8,128)(2,1)}, bf16[2048,1024]{1,0:T(8,128)(2,1)}, u32[]{:S(2)}, u32[]{:S(2)}) %collective-permute-start.2) | collective-permute-done | bytes 4194336 | tf_op jit(solution)/shard_map/ppermute | solution.py:197
  385.7 4.7 constant_dynamic-update-slice_fusion.4
  394.1 4.7 constant_dynamic-update-slice_fusion
  398.8 7.0 add_bitcast_fusion.1
  410.0 5.9 copy.132
  415.8 5.6 reshape.344
  421.5 5.7 reshape.345
  427.2 9.9 fusion.205
  437.0 5.2 copy.199
  442.2 6.4 copy.200
  448.6 10.1 fusion.204
  458.7 6.4 copy.197
  465.1 6.4 copy.198
  471.5 7.1 add_bitcast_fusion
  482.6 5.6 reshape.346
  488.2 5.6 reshape.347
  493.8 9.7 fusion.203
  503.6 6.4 copy.203
  510.0 6.4 copy.204
  516.4 9.9 fusion.202
  526.3 6.4 copy.201
  532.7 6.6 copy.202
  539.3 5.8 subtract_convert_fusion.3
  560.8 4.3 fusion.113
  565.1 4.1 fusion
  569.3 4.3 exponential_reduce_fusion
  574.8 4.2 fusion.112
  585.7 25.0 %all-to-all-done = bf16[8,512,128]{1,2,0:T(8,128)(2,1)S(1)} async-done(((bf16[8,512,128]{1,2,0:T(8,128)(2,1)}), bf16[8,512,128]{1,2,0:T(8,128)(2,1)S(1)}, u32[]{:S(2)}, u32[]{:S(2)}) %all-to-all-start) | async-done | bytes 1048608 | tf_op jit(solution)/shard_map/all_to_all | solution.py:207
  620.2 123.5 %all-gather.7.cloned.1.call-done = bf16[4096,1024]{1,0:T(8,128)(2,1)} async-done(((bf16[512,1024]{1,0:T(8,128)(2,1)}), bf16[4096,1024]{1,0:T(8,128)(2,1)}) %all-gather.7.cloned.1.call-update) | async-done | bytes 8388624 | tf_op jit(solution)/shard_map/all_gather | solution.py:214
  743.6 10.0 multiply_convert_fusion.3
  755.6 6.7 convolution_convert_fusion.1
  763.1 145.0 %reduce-scatter.5.cloned.1.call-done = bf16[512,1024]{1,0:T(8,128)(2,1)} async-done(((bf16[4096,1024]{1,0:T(8,128)(2,1)}), bf16[512,1024]{1,0:T(8,128)(2,1)}) %reduce-scatter.5.cloned.1.call-update) | async-done | bytes 1048592 | tf_op jit(solution)/shard_map/reduce_scatter | solution.py:218
  917.4 123.6 %all-gather.9.cloned.1.call-done = bf16[4096,1024]{1,0:T(8,128)(2,1)} async-done(((bf16[512,1024]{1,0:T(8,128)(2,1)}), bf16[4096,1024]{1,0:T(8,128)(2,1)}) %all-gather.9.cloned.1.call-update) | async-done | bytes 8388624 | tf_op jit(solution)/shard_map/all_gather | solution.py:250
  1041.0 12.5 fusion.209
  1055.5 7.2 convolution_convert_fusion
  1065.5 5.0 reshape.348
  1070.5 5.9 copy.155
  1077.5 5.8 fusion.187
  1086.0 8.1 fusion.123
  1094.1 114.5 %reduce-scatter.7.cloned.1.call-done = bf16[512,1024]{1,0:T(8,128)(2,1)} async-done(((bf16[4096,1024]{1,0:T(8,128)(2,1)}), bf16[512,1024]{1,0:T(8,128)(2,1)}) %reduce-scatter.7.cloned.1.call-update) | async-done | bytes 1048592 | tf_op jit(solution)/shard_map/reduce_scatter | solution.py:266
  1208.6 5.2 fusion.76
  1225.6 10.3 convolution_convert_fusion.3
  1235.9 8.2 convolution_convert_fusion.4
  1246.7 4.7 all-to-all-done.1
  1256.2 4.5 fusion.101
  1281.5 8.0 multiply_reduce_fusion.1
  1289.8 7.1 fusion.44
  1298.6 9.3 multiply_convert_fusion.1
  1307.9 5.8 fusion.43
  1313.7 5.8 fusion.99
  1319.5 11.4 multiply_reduce_fusion
  1330.9 7.9 fusion.55
  1338.8 6.1 copy.181
  1344.9 4.7 reshape.342
  1349.7 12.4 multiply_convert_fusion
  1382.4 7.0 fusion.96
  1389.5 8.8 bitcast_convert_fusion
  1400.8 6.5 all-reduce.7
  1408.5 48.6 %all-reduce.11.cloned.1.call-done = (bf16[3,1024,128]{1,2,0:T(8,128)(2,1)}, bf16[128,1024]{1,0:T(8,128)(2,1)}, bf16[1024,512]{1,0:T(8,128)(2,1)}, bf16[512,1024]{1,0:T(8,128)(2,1)}) async-done(((bf16[3,1024,128]{1,2,0:T(8,128)(2,1)}, bf16[128,1024]{1,0:T(8,128)(2,1)}, bf16[1024,512]{1,0:T(8,128)(2,1)}, bf16[512,1024]{1,0:T(8,128)(2,1)}), (bf16[3,1024,128]{1,2,0:T(8,128)(2,1)}, bf16[128,1024]{1,0:T(8,128)(2,1)}, ...) | async-done | bytes 3145744 | tf_op jit(solution)/shard_map/psum | solution.py:339
  1466.1 142.2 %reduce-scatter.9.cloned.1.call-done = bf16[512,1024]{1,0:T(8,128)(2,1)} async-done(((bf16[4096,1024]{1,0:T(8,128)(2,1)}), bf16[512,1024]{1,0:T(8,128)(2,1)}) %reduce-scatter.9.cloned.1.call-update) | async-done | bytes 1048592 | tf_op jit(solution)/shard_map/reduce_scatter | solution.py:309
  1610.7 40.3 %all-reduce.6 = (f32[1024]{0:T(1024)}, f32[1024]{0:T(1024)}, f32[4,1024]{1,0:T(4,128)}, f32[4,1024]{1,0:T(4,128)}) all-reduce(f32[1024]{0:T(1024)S(1)} %copy-done.82, f32[1024]{0:T(1024)S(1)} %copy-done.78, f32[4,1024]{1,0:T(4,128)S(1)} %pad_maximum_fusion.15, ...), channel_id=1, replica_groups=mesh['wide'=4,'narrow'=8] {'wide','narrow'}, use_global_device_ids=true, to_apply=%region_39.40 | all-reduce | flops 10240 | bytes 81920 | tf_op jit(solution)/shard_map/psum | solution.py:346
  (346 shorter events, 171.1 us)
Async XLA Ops:
  7.2 736.5 %copy-start = (bf16[1024,512]{1,0:T(8,128)(2,1)S(1)}, bf16[1024,512]{1,0:T(8,128)(2,1)}, u32[]{:S(2)}) copy-start(bf16[1024,512]{1,0:T(8,128)(2,1)} %param.22) | copy-start | bytes 3145732
  7.2 464.4 %all-gather.11.cloned.1.call-start = ((), (), s32[]{:S(2)}) async-start(), calls=%async_computation.11 | async-start | bytes 9437184 | tf_op jit(solution)/shard_map/all_gather | solution.py:278
  8.8 7.6 copy-start.73
  16.4 108.8 %copy-start.22 = (bf16[512,1024]{1,0:T(8,128)(2,1)S(1)}, bf16[512,1024]{1,0:T(8,128)(2,1)}, u32[]{:S(2)}) copy-start(bf16[512,1024]{1,0:T(8,128)(2,1)} %get-tuple-element.94) | copy-start | bytes 3145732
  16.4 569.3 %all-gather.5.cloned.1.call-start = ((), (), s32[]{:S(2)}) async-start(), calls=%async_computation.6 | async-start | bytes 2359296 | tf_op jit(solution)/shard_map/all_gather | solution.py:208
  16.5 46.7 %collective-permute-start = (bf16[512,1024]{1,0:T(8,128)(2,1)}, bf16[512,1024]{1,0:T(8,128)(2,1)S(1)}, u32[]{:S(2)}, u32[]{:S(2)}) collective-permute-start(bf16[512,1024]{1,0:T(8,128)(2,1)} %get-tuple-element.94), channel_id=1, source_target_pairs={{0,7},{1,0},{2,1},{3,2},{4,3},{5,4},{6,5},{7,6},{8,15},{9,8},{10,9... | collective-permute-start | bytes 3145736 | tf_op jit(solution)/shard_map/ppermute | solution.py:197
  63.1 64.4 %copy-start.26 = (bf16[512,1024]{1,0:T(8,128)(2,1)}, bf16[512,1024]{1,0:T(8,128)(2,1)S(1)}, u32[]{:S(2)}) copy-start(bf16[512,1024]{1,0:T(8,128)(2,1)S(1)} %collective-permute-done) | copy-start | bytes 3145732
  65.0 58.8 %collective-permute-start.1 = (bf16[1024,1024]{1,0:T(8,128)(2,1)S(1)}, bf16[1024,1024]{1,0:T(8,128)(2,1)S(1)}, u32[]{:S(2)}, u32[]{:S(2)}) collective-permute-start(bf16[1024,1024]{1,0:T(8,128)(2,1)S(1)} %pad_maximum_fusion.1), channel_id=1, source_target_pairs={{0,6},{1,7},{2,0},{3,1},{4,2},{5,3},{6,4},{7,5},{8,14},{9,15},{10,... | collective-permute-start | bytes 6291464 | tf_op jit(solution)/shard_map/ppermute | solution.py:197
  127.5 258.2 %collective-permute-start.2 = (bf16[2048,1024]{1,0:T(8,128)(2,1)}, bf16[2048,1024]{1,0:T(8,128)(2,1)}, u32[]{:S(2)}, u32[]{:S(2)}) collective-permute-start(bf16[2048,1024]{1,0:T(8,128)(2,1)} %pad_maximum_fusion), channel_id=1, source_target_pairs={{0,4},{1,5},{2,6},{3,7},{4,0},{5,1},{6,2},{7,3},{8,12},{9,13},{10,... | collective-permute-start | bytes 12582920 | tf_op jit(solution)/shard_map/ppermute | solution.py:197
  129.0 7.9 copy-start.25
  134.3 440.5 %copy-start.18 = (pred[512,2048]{1,0:T(8,128)(4,1)}, pred[512,2048]{1,0:T(8,128)(4,1)S(1)}, u32[]{:S(2)}) copy-start(pred[512,2048]{1,0:T(8,128)(4,1)S(1)} %iota_compare_fusion) | copy-start | bytes 3145732
  138.4 253.0 %copy-start.27 = (bf16[512,1024]{1,0:T(8,128)(2,1)S(1)}, bf16[512,1024]{1,0:T(8,128)(2,1)}, u32[]{:S(2)}) copy-start(bf16[512,1024]{1,0:T(8,128)(2,1)} %copy-done.26) | copy-start | bytes 3145732
  545.1 6.1 copy-start.51
  545.1 6.1 copy-start.53
  545.1 6.1 copy-start.54
  579.2 32.5 %copy-start.66 = (f32[1024]{0:T(1024)S(1)}, f32[1024]{0:T(1024)}, u32[]{:S(2)}) copy-start(f32[1024]{0:T(1024)} %param.21) | copy-start | bytes 12292
  582.1 28.7 %all-to-all-start = ((bf16[8,512,128]{1,2,0:T(8,128)(2,1)}), bf16[8,512,128]{1,2,0:T(8,128)(2,1)S(1)}, u32[]{:S(2)}, u32[]{:S(2)}) async-start(bf16[8,512,128]{1,2,0:T(8,128)(2,1)} %copy.144), calls=%async_computation | async-start | bytes 2097152 | tf_op jit(solution)/shard_map/all_to_all | solution.py:207
  585.7 158.0 %all-gather.7.cloned.1.call-start = ((), (), s32[]{:S(2)}) async-start(), calls=%async_computation.7 | async-start | bytes 9437184 | tf_op jit(solution)/shard_map/all_gather | solution.py:214
  617.4 126.2 %copy-start.93 = (f32[512]{0:T(512)S(1)}, f32[512]{0:T(512)}, u32[]{:S(2)}) copy-start(f32[512]{0:T(512)} %param.23) | copy-start | bytes 6148
  620.1 288.0 %reduce-scatter.5.cloned.1.call-start = ((), (), s32[]{:S(2)}) async-start(), calls=%async_computation.8 | async-start | bytes 9437184 | tf_op jit(solution)/shard_map/reduce_scatter | solution.py:218
  743.6 12.0 copy-start.89
  762.3 145.9 %copy-start.67 = (f32[1024]{0:T(1024)S(1)}, f32[1024]{0:T(1024)}, u32[]{:S(2)}) copy-start(f32[1024]{0:T(1024)} %param.25) | copy-start | bytes 12292
  762.3 149.2 %copy-start.72 = (f32[1,1024]{1,0:T(1,128)S(1)}, f32[1,1024]{1,0:T(1,128)}, u32[]{:S(2)}) copy-start(f32[1,1024]{1,0:T(1,128)} %get-tuple-element.132) | copy-start | bytes 12292
  762.3 278.7 %all-gather.9.cloned.1.call-start = ((), (), s32[]{:S(2)}) async-start(), calls=%async_computation.9 | async-start | bytes 9437184 | tf_op jit(solution)/shard_map/all_gather | solution.py:250
  908.2 6.7 copy-start.21
  908.2 6.7 copy-start.33
  917.3 291.2 %reduce-scatter.7.cloned.1.call-start = ((), (), s32[]{:S(2)}) async-start(), calls=%async_computation.10 | async-start | bytes 9437184 | tf_op jit(solution)/shard_map/reduce_scatter | solution.py:266
  1062.7 13.7 copy-start.8
  1062.7 13.7 copy-start.9
  1077.4 8.5 copy-start.43
  1086.0 122.6 %copy-start.83 = (f32[1,1024]{1,0:T(1,128)S(1)}, f32[1,1024]{1,0:T(1,128)}, u32[]{:S(2)}) copy-start(f32[1,1024]{1,0:T(1,128)} %get-tuple-element.136) | copy-start | bytes 12292
  1221.9 29.6 %all-to-all-start.1 = ((bf16[512,8,128]{0,2,1:T(8,128)(2,1)}), bf16[512,8,128]{0,2,1:T(8,128)(2,1)S(1)}, u32[]{:S(2)}, u32[]{:S(2)}) async-start(bf16[512,8,128]{0,2,1:T(8,128)(2,1)} %bitcast.18), calls=%async_computation.3 | async-start | bytes 2097152 | tf_op jit(solution)/shard_map/all_to_all | solution.py:285
  1225.5 163.9 %reduce-scatter.11.cloned.1.call-start = ((), (), s32[]{:S(2)}) async-start(), calls=%async_computation.13 | async-start | bytes 2359296 | tf_op jit(solution)/shard_map/reduce_scatter | solution.py:293
  1225.6 10.3 copy-start.96
  1235.9 8.2 copy-start.39
  1235.9 8.2 copy-start.63
  1246.7 210.4 %all-reduce.11.cloned.1.call-start = ((), (), s32[]{:S(2)}) async-start(), calls=%async_computation.14 | async-start | bytes 6291456 | tf_op jit(solution)/shard_map/psum | solution.py:339
  1254.6 6.0 copy-start.6
  1254.7 6.0 copy-start.30
  1281.5 8.3 copy-start.2
  1289.8 8.8 copy-start.3
  1298.6 20.9 %slice-start = ((s8[16777216]{0:T(1024)(128)(4,1)}), s8[4194304]{0:T(1024)(128)(4,1)S(1)}, s32[]{:S(2)}) async-start(s8[16777216]{0:T(1024)(128)(4,1)} %bitcast.124), calls=%async_computation.15 | async-start | bytes 8388608
  1298.6 20.9 %slice-start.1 = ((s8[16777216]{0:T(1024)(128)(4,1)}), s8[4194304]{0:T(1024)(128)(4,1)S(1)}, s32[]{:S(2)}) async-start(s8[16777216]{0:T(1024)(128)(4,1)} %bitcast.124), calls=%async_computation.16 | async-start | bytes 8388608
  1298.6 20.9 %slice-start.2 = ((s8[16777216]{0:T(1024)(128)(4,1)}), s8[4194304]{0:T(1024)(128)(4,1)S(1)}, s32[]{:S(2)}) async-start(s8[16777216]{0:T(1024)(128)(4,1)} %bitcast.124), calls=%async_computation.17 | async-start | bytes 8388608
  1307.9 11.6 slice-start.3
  1338.8 10.8 copy-start.20
  1338.8 10.8 copy-start.77
  1349.7 12.4 copy-start.13
  1349.7 12.4 copy-start.17
  1382.4 7.1 copy-start.91
  1389.4 218.8 %reduce-scatter.9.cloned.1.call-start = ((), (), s32[]{:S(2)}) async-start(), calls=%async_computation.12 | async-start | bytes 9437184 | tf_op jit(solution)/shard_map/reduce_scatter | solution.py:309
  1457.1 7.4 copy-start.61
  1459.0 149.3 %copy-start.7 = (bf16[512,1024]{1,0:T(8,128)(2,1)S(1)}, bf16[512,1024]{1,0:T(8,128)(2,1)}, u32[]{:S(2)}) copy-start(bf16[512,1024]{1,0:T(8,128)(2,1)} %param.14) | copy-start | bytes 3145732
  1459.0 149.3 %copy-start.71 = (f32[1,1024]{1,0:T(1,128)S(1)}, f32[1,1024]{1,0:T(1,128)}, u32[]{:S(2)}) copy-start(f32[1,1024]{1,0:T(1,128)} %copy-done.70) | copy-start | bytes 12292
  1459.0 149.3 %copy-start.74 = (f32[512]{0:T(512)S(1)}, f32[512]{0:T(512)}, u32[]{:S(2)}) copy-start(f32[512]{0:T(512)} %copy-done.73) | copy-start | bytes 6148
  1459.0 149.3 %copy-start.76 = (f32[512]{0:T(512)S(1)}, f32[512]{0:T(512)}, u32[]{:S(2)}) copy-start(f32[512]{0:T(512)} %copy-done.75) | copy-start | bytes 6148
  1461.6 148.9 %copy-start.80 = (f32[1024]{0:T(1024)S(1)}, f32[1024]{0:T(1024)}, u32[]{:S(2)}) copy-start(f32[1024]{0:T(1024)} %get-tuple-element.64) | copy-start | bytes 12292
  1461.6 149.0 %copy-start.81 = (f32[1024]{0:T(1024)S(1)}, f32[1024]{0:T(1024)}, u32[]{:S(2)}) copy-start(f32[1024]{0:T(1024)} %get-tuple-element.60) | copy-start | bytes 12292
  1461.6 149.0 %copy-start.85 = (f32[1024]{0:T(1024)S(1)}, f32[1024]{0:T(1024)}, u32[]{:S(2)}) copy-start(f32[1024]{0:T(1024)} %get-tuple-element.62) | copy-start | bytes 12292
  1461.6 149.0 %copy-start.79 = (f32[1024]{0:T(1024)S(1)}, f32[1024]{0:T(1024)}, u32[]{:S(2)}) copy-start(f32[1024]{0:T(1024)} %get-tuple-element.73) | copy-start | bytes 12292
  1461.6 149.0 %copy-start.84 = (f32[1024]{0:T(1024)S(1)}, f32[1024]{0:T(1024)}, u32[]{:S(2)}) copy-start(f32[1024]{0:T(1024)} %get-tuple-element.75) | copy-start | bytes 12292
  1461.6 149.0 %copy-start.78 = (f32[1024]{0:T(1024)S(1)}, f32[1024]{0:T(1024)}, u32[]{:S(2)}) copy-start(f32[1024]{0:T(1024)} %get-tuple-element.86) | copy-start | bytes 12292
  1461.6 149.0 %copy-start.82 = (f32[1024]{0:T(1024)S(1)}, f32[1024]{0:T(1024)}, u32[]{:S(2)}) copy-start(f32[1024]{0:T(1024)} %get-tuple-element.88) | copy-start | bytes 12292
  1464.5 190.1 %copy-start.1 = (bf16[1024,512]{1,0:T(8,128)(2,1)S(1)}, bf16[1024,512]{1,0:T(8,128)(2,1)}, u32[]{:S(2)}) copy-start(bf16[1024,512]{1,0:T(8,128)(2,1)} %param.22) | copy-start | bytes 3145732
  (53 other events, 164.7 us)
Sparse Core Ops, SparseCore 0:
  16.5 306.6 all-gather.10
  325.3 85.9 all-gather.4
  620.2 123.3 all-gather.6
  762.5 145.6 reduce-scatter.4
  917.5 123.5 all-gather.8
  1062.8 145.6 reduce-scatter.6
  1246.8 69.7 reduce-scatter.10
  1389.6 67.4 all-reduce.10
  1460.7 147.5 reduce-scatter.8
